TPU v7x, 32 devices: a whole 2x2x4 slice. The times are simulated.
32 devices in a mesh: walk: 4 (over x, core), chol: 8 (over z, y).
Axes of the slice: x: 2, y: 2, z: 4, core: 2. Of those that a mesh axis runs over, the one named last changes fastest.
Arguments:
- old_walkers: bfloat16 [96, 2048, 128], P(('walk', 'chol'))
- half_chol: bfloat16 [16, 128, 2048], P('chol'), may hold values from -0.1875 to 0.1875
- parent: int32 [192], P(('walk', 'chol')), may hold values from -1 to 11, as said below
- field: float32 [192, 2048], P(('walk', 'chol')), may hold values from -0.8 to 0.8
Outputs:
- new_walkers: bfloat16 [192, 2048, 128], P(('walk', 'chol'))
- energy: float32 [192], P(('walk', 'chol'))
Inputs may be any that keep to these rules, and one draw needn't show every extreme that they name: `parent`: the 4 devices that share an index of chol form a column. On each device the live slots (value >= 0) come first among its 6 slots, the rest hold -1. Each column has exactly 12 live slots, every device of it at least one, and some device of it has all 6 slots live. A live value m names the walker that the column's walk index m // 3 holds as its local walker m % 3.
All inputs are finite; a program needn't handle non-finite values.
Results may differ from a plain program's by a relative error of at most 0.0062.
Values may be sent and summed in bfloat16 or wider, within the bound.
No kernel may reach another device: no remote copies, remote signals or barrier semaphores. Data moves between devices by JAX's collectives and lax.ppermute only.
A program may use at most 192 MiB of HBM per device.

v0:
```python
import jax
import jax.numpy as jnp
from jax import lax
from jax.sharding import PartitionSpec as P

ITERS = 3


def green_half(walkers):
    widened = walkers.astype(jnp.float32)
    electrons = walkers.shape[2]
    intersection = widened[:, :electrons, :]
    identity = jnp.eye(electrons, dtype=jnp.float32)
    diagonal = jnp.diagonal(intersection, axis1=1, axis2=2)
    inverse = identity[None, :, :] / diagonal[:, None, :]
    for sweep in range(ITERS):
        product = jnp.einsum("wij,wjk->wik", intersection, inverse, precision=lax.Precision.HIGHEST)
        inverse = jnp.einsum(
            "wij,wjk->wik",
            inverse,
            2.0 * identity[None, :, :] - product,
            precision=lax.Precision.HIGHEST,
        )
    theta = jnp.einsum("wnk,wkj->wnj", widened, inverse, precision=lax.Precision.HIGHEST)
    return theta.astype(jnp.bfloat16)


def block_energy(theta, vectors):
    blocks = jnp.einsum("gin,wnj->wgij", vectors, theta, preferred_element_type=jnp.float32)
    traces = jnp.einsum("wgii->wg", blocks)
    crossed = jnp.sum(blocks * jnp.swapaxes(blocks, 2, 3), axis=(2, 3))
    return 0.5 * jnp.sum(traces * traces - crossed, axis=1)


def body(old_walkers, half_chol, parent, field):
    slot_dev = parent.shape[0]
    column = lax.all_gather(old_walkers, "walk", axis=0, tiled=True)
    living = parent >= 0
    source = jnp.maximum(parent, 0)
    kicked = (jnp.exp(field)[:, :, None] * column[source].astype(jnp.float32)).astype(jnp.bfloat16)
    new_walkers = jnp.where(living[:, None, None], kicked, jnp.zeros_like(kicked))
    theta = green_half(kicked)
    energy = jnp.zeros((slot_dev,), jnp.float32) + block_energy(
        theta, lax.all_gather(half_chol, "chol", axis=0, tiled=True)
    )
    energy = jnp.where(living, energy, 0.0)
    return (new_walkers, energy)


def solution(mesh):
    return jax.shard_map(
        body,
        mesh=mesh,
        in_specs=(
            P(("walk", "chol"), None, None),
            P("chol", None, None),
            P(("walk", "chol")),
            P(("walk", "chol"), None),
        ),
        out_specs=(P(("walk", "chol"), None, None), P(("walk", "chol"))),
        check_vma=False,
    )
```

profile of v0, /device:TPU:0, one launch (start us, length us, event | category | flops | bytes accessed | tf_op | source)
XLA Modules:
  0.0 217.5 jit_solution(15850261391445615935)
XLA Ops:
  7.2 0.0 all-gather.3.cloned.1.call-start
  7.2 0.7 all-gather.3.cloned.1.call-update
  7.9 0.0 all-gather.5.cloned.1.call-start
  7.9 0.7 all-gather.5.cloned.1.call-update
  8.6 0.9 exp.3
  9.5 0.7 broadcast_maximum_fusion
  10.2 0.6 iota_compare_fusion.1
  10.8 0.6 fusion.15
  11.4 0.7 fusion.16
  12.1 0.7 broadcast_compare_fusion
  12.7 45.9 %all-gather.3.cloned.1.call-done = bf16[12,2048,128]{2,1,0:T(8,128)(2,1)} async-done(((bf16[3,2048,128]{2,1,0:T(8,128)(2,1)}), bf16[12,2048,128]{2,1,0:T(8,128)(2,1)}) %all-gather.3.cloned.1.call-update) | async-done | bytes 6291472 | tf_op jit(solution)/shard_map/all_gather | solution.py:37
  58.7 5.5 %gather_fusion = bf16[6,2048,128]{2,1,0:T(8,128)(2,1)} fusion(bf16[12,2048,128]{2,1,0:T(8,128)(2,1)} %all-gather.3.cloned.1.call-done, s32[1024]{0:T(1024)S(1)} %pad_clamp_fusion), kind=kCustom, calls=%fused_computation | custom fusion | bytes 6291480 | tf_op jit(solution)/shard_map/gather | solution.py:40
  64.2 5.1 %broadcast_select_fusion = (bf16[6,2048,128]{2,1,0:T(8,128)(2,1)}, bf16[6,2048,128]{2,1,0:T(8,128)(2,1)S(1)}) fusion(pred[6]{0:T(512)(128)(4,1)S(1)} %broadcast_compare_fusion, bf16[6,2048,128]{2,1,0:T(8,128)(2,1)} %gather_fusion, f32[6,2048]{1,0:T(8,128)S(1)} %exp.3), kind=kLoop, calls=%fused_computation.11 | loop fusion | flops 6291456 | bytes 9486342 | tf_op jit(solution)/shard_map/jit(_where)/select_n | solution.py:41
  69.3 4.7 %copy.17 = f32[6,128,128]{0,2,1:T(8,128)} copy(f32[6,128,128]{2,1,0:T(8,128)S(1)} %slice_convert_fusion) | data formatting | bytes 786432 | tf_op jit(solution)/shard_map/slice | solution.py:12
  74.0 0.0 copy-start
  74.0 1.8 gather_fusion.1
  75.8 0.1 copy.18
  75.8 1.3 convolution_subtract_fusion.2
  77.1 1.4 fusion.5
  78.5 0.0 copy-done
  78.5 0.3 convolution_subtract_fusion.1
  78.9 0.5 fusion.17
  79.4 0.3 convolution_subtract_fusion
  79.7 0.5 fusion.18
  80.3 4.0 %convolution_convert_fusion = bf16[6,2048,128]{2,1,0:T(8,128)(2,1)} fusion(bf16[6,2048,128]{2,1,0:T(8,128)(2,1)S(1)} %get-tuple-element.7, f32[6,128,128]{2,1,0:T(8,128)S(1)} %fusion.18), kind=kOutput, calls=%fused_computation.9 | convolution fusion | flops 2417491968 | bytes 6684672 | tf_op jit(solution)/shard_map/wnk,wkj->wnj/dot_general | solution.py:24
  84.2 101.5 %all-gather.5.cloned.1.call-done = bf16[16,128,2048]{2,1,0:T(8,128)(2,1)} async-done(((bf16[2,128,2048]{2,1,0:T(8,128)(2,1)}), bf16[16,128,2048]{2,1,0:T(8,128)(2,1)}) %all-gather.5.cloned.1.call-update) | async-done | bytes 8388624 | tf_op jit(solution)/shard_map/all_gather | solution.py:44
  185.8 11.7 %fusion = f32[6,128,16,128]{3,1,2,0:T(8,128)} fusion(bf16[16,128,2048]{2,1,0:T(8,128)(2,1)} %all-gather.5.cloned.1.call-done, bf16[6,2048,128]{2,1,0:T(8,128)(2,1)} %convolution_convert_fusion), kind=kOutput, calls=%fused_computation.2 | convolution fusion | flops 6442450944 | bytes 17825792 | tf_op jit(solution)/shard_map/gin,wnj->wgij/dot_general | solution.py:29
  197.5 0.0 copy-start.1
  197.5 6.6 %copy.20 = f32[6,128,16,128]{1,3,2,0:T(8,128)} copy(f32[6,128,16,128]{3,1,2,0:T(8,128)} %fusion) | data formatting | bytes 12582912 | tf_op jit(solution)/shard_map/gin,wnj->wgij/dot_general | solution.py:29
  204.1 0.0 copy-done.1
  204.1 0.0 copy-start.2
  204.1 5.9 %fusion.3 = (f32[6,16]{1,0:T(8,128)S(1)}, f32[6,16]{1,0:T(8,128)S(1)}) fusion(f32[6,128,16,128]{1,3,2,0:T(8,128)} %copy.20, pred[128,128]{1,0:T(8,128)(4,1)S(1)} %copy-done.1, f32[6,128,16,128]{3,1,2,0:T(8,128)} %fusion), kind=kLoop, calls=%fused_computation.7 | loop fusion | flops 6291264 | bytes 12600064 | tf_op jit(solution)/shard_map/wgii->wg/reduce_sum | solution.py:30
  210.0 0.1 subtract_reduce_fusion
  210.1 0.0 copy-done.2
  210.1 0.5 multiply_select_fusion
  (3 shorter events, 0.0 us)
Async XLA Ops:
  7.2 51.5 %all-gather.3.cloned.1.call-start = ((), (), s32[]{:S(2)}) async-start(), calls=%async_computation | async-start | bytes 7864320 | tf_op jit(solution)/shard_map/all_gather | solution.py:37
  7.9 177.9 %all-gather.5.cloned.1.call-start = ((), (), s32[]{:S(2)}) async-start(), calls=%async_computation.1 | async-start | bytes 9437184 | tf_op jit(solution)/shard_map/all_gather | solution.py:44
  74.0 4.5 %copy-start = (f32[128,128]{1,0:T(8,128)S(1)}, f32[128,128]{1,0:T(8,128)}, u32[]{:S(2)}) copy-start(f32[128,128]{1,0:T(8,128)} %fusion.15) | copy-start | bytes 196612
  197.5 6.6 %copy-start.1 = (pred[128,128]{1,0:T(8,128)(4,1)S(1)}, pred[128,128]{1,0:T(8,128)(4,1)}, u32[]{:S(2)}) copy-start(pred[128,128]{1,0:T(8,128)(4,1)} %iota_compare_fusion.1) | copy-start | bytes 49156
  204.1 6.0 %copy-start.2 = (s32[6]{0:T(128)S(1)}, s32[6]{0:T(128)}, u32[]{:S(2)}) copy-start(s32[6]{0:T(128)} %param.6) | copy-start | bytes 76
Sparse Core Ops, SparseCore 0:
  9.6 49.0 all-gather.2
  60.8 124.9 all-gather.4
where the time goes:
time: 218 us; the launch traced here: 217 us
  waiting for transfers between devices  149 us (68%)
  matrix products  20.1 us (9%)
  local copies, waits for them, and re-layouts  19.5 us (9%)
  other arithmetic  14.8 us (7%)
  between operations  14.1 us (6%)
    all_gather x1, waiting for transfers between devices, body(): lax.all_gather(half_chol, 'chol', axis=0, tiled=True)  102 us
    all_gather x1, waiting for transfers between devices, body(): column = lax.all_gather(old_walkers, 'walk', axis=0, tiled=True)  45.9 us
    dot_general x1, matrix products, block_energy(): jnp.einsum('gin,wnj->wgij', vectors, theta, preferred_element_type=jnp.fl...  11.7 us
    dot_general x1, local copies, waits for them, and re-layouts, block_energy(): jnp.einsum('gin,wnj->wgij', vectors, theta, preferred_element_type=jnp.fl...  6.6 us
    reduce_sum x1, other arithmetic, block_energy(): traces = jnp.einsum('wgii->wg', blocks)  5.87 us
    gather x1, local copies, waits for them, and re-layouts, body(): column[source].astype(jnp.float32)  5.5 us
    select_n x1, other arithmetic, body(): jnp.where(living[:, None, None], kicked, jnp.zeros_like(kicked))  5.09 us
    slice x1, local copies, waits for them, and re-layouts, green_half(): intersection = widened[:, :electrons, :]  4.72 us
  transfers between devices with their start and end apart: 2, of which 2 were waited for; matrix products, arithmetic and copies ran while one was open for 14% of the time, Pallas kernels for 0%

commit v1 on v0

--- a/solution.py
+++ b/solution.py
@@ -4,6 +4,19 @@
 from jax.sharding import PartitionSpec as P
 
 ITERS = 3
+
+
+def _place_racks(page, dim_at):
+    lanes = lax.axis_size("walk")
+    seen_now = page
+    store = [seen_now]
+    even = [(num - 1, num) for num in range(1, lanes)] + [(lanes - 1, 0)]
+    for _ in range(lanes - 1):
+        seen_now = lax.ppermute(seen_now, "walk", even)
+        store += [seen_now]
+    formed = jnp.concatenate([*reversed(store)], dim_at)
+    d_next = lax.axis_index("walk")
+    return jnp.roll(formed, (d_next + 1) * seen_now.shape[dim_at], dim_at)
 
 
 def green_half(walkers):
@@ -34,7 +47,7 @@
 
 def body(old_walkers, half_chol, parent, field):
     slot_dev = parent.shape[0]
-    column = lax.all_gather(old_walkers, "walk", axis=0, tiled=True)
+    column = _place_racks(old_walkers, 0)
     living = parent >= 0
     source = jnp.maximum(parent, 0)
     kicked = (jnp.exp(field)[:, :, None] * column[source].astype(jnp.float32)).astype(jnp.bfloat16)

time: 218 us -> 170 us (0.78)
  waiting for transfers between devices: 149 us -> 88.3 us
  local copies, waits for them, and re-layouts: 19.5 us -> 29.9 us
    all_gather x1, waiting for transfers between devices: 102 us -> 31.4 us  [body(): lax.all_gather(half_chol, 'chol', axis=0, tiled=True)]
    ppermute x0 -> x3, waiting for transfers between devices: none -> 56.2 us  [_place_racks(): seen_now = lax.ppermute(seen_now, 'walk', even)]
    all_gather x1 -> x0, waiting for transfers between devices: 45.9 us -> none  [body(): column = lax.all_gather(old_walkers, 'walk', axis=0, tiled=True)]
    unnamed x6 -> x13, local copies, waits for them, and re-layouts: 0.01 us -> 6.99 us
    dynamic_slice x0 -> x1, local copies, waits for them, and re-layouts: none -> 3.14 us  [_place_racks(): return jnp.roll(formed, (d_next + 1) * seen_now.shape[dim_at], dim_at)]
  transfers between devices with their start and end apart: 2 -> 4, of which waited for: 2 -> 4; matrix products, arithmetic and copies ran while one was open for 14% -> 25% of each run, Pallas kernels for 0% -> 0%
where the time goes in v1:
time: 170 us
  waiting for transfers between devices  88.3 us (52%)
  local copies, waits for them, and re-layouts  29.9 us (18%)
  matrix products  21.7 us (13%)
  other arithmetic  14.8 us (9%)
  between operations  14.2 us (8%)
    ppermute x3, waiting for transfers between devices, _place_racks(): seen_now = lax.ppermute(seen_now, 'walk', even)  56.2 us
    all_gather x1, waiting for transfers between devices, body(): lax.all_gather(half_chol, 'chol', axis=0, tiled=True)  31.4 us
    dot_general x1, matrix products, block_energy(): jnp.einsum('gin,wnj->wgij', vectors, theta, preferred_element_type=jnp.fl...  11.7 us
    unnamed x13, local copies, waits for them, and re-layouts  6.99 us
    dot_general x1, local copies, waits for them, and re-layouts, block_energy(): jnp.einsum('gin,wnj->wgij', vectors, theta, preferred_element_type=jnp.fl...  6.6 us
    reduce_sum x1, other arithmetic, block_energy(): traces = jnp.einsum('wgii->wg', blocks)  5.87 us
    gather x1, local copies, waits for them, and re-layouts, body(): column[source].astype(jnp.float32)  5.55 us
    select_n x1, other arithmetic, body(): jnp.where(living[:, None, None], kicked, jnp.zeros_like(kicked))  5.05 us
  transfers between devices with their start and end apart: 4, of which 4 were waited for; matrix products, arithmetic and copies ran while one was open for 25% of the time, Pallas kernels for 0%

profile of v1, /device:TPU:0, one launch (start us, length us, event | category | flops | bytes accessed | tf_op | source)
XLA Modules:
  0.0 169.5 jit_solution(13644167803137013342)
XLA Ops:
  7.2 0.0 copy-start
  7.2 0.0 all-gather.2.cloned.1.call-start
  7.2 0.7 all-gather.2.cloned.1.call-update
  7.9 0.5 collective-permute-start
  8.4 20.2 %collective-permute-done = bf16[3,2048,128]{2,1,0:T(8,128)(2,1)S(1)} collective-permute-done((bf16[3,2048,128]{2,1,0:T(8,128)(2,1)}, bf16[3,2048,128]{2,1,0:T(8,128)(2,1)S(1)}, u32[]{:S(2)}, u32[]{:S(2)}) %collective-permute-start) | collective-permute-done | bytes 1572896 | tf_op jit(solution)/shard_map/ppermute | solution.py:15
  28.6 0.0 collective-permute-start.1
  28.7 19.9 %collective-permute-done.1 = bf16[3,2048,128]{2,1,0:T(8,128)(2,1)} collective-permute-done((bf16[3,2048,128]{2,1,0:T(8,128)(2,1)S(1)}, bf16[3,2048,128]{2,1,0:T(8,128)(2,1)}, u32[]{:S(2)}, u32[]{:S(2)}) %collective-permute-start.1) | collective-permute-done | bytes 1572896 | tf_op jit(solution)/shard_map/ppermute | solution.py:15
  48.6 0.0 collective-permute-start.2
  48.6 0.9 exp.3
  49.5 0.7 broadcast_maximum_fusion
  50.1 0.6 iota_compare_fusion.1
  50.8 0.6 fusion.15
  51.4 0.7 fusion.16
  52.0 0.7 broadcast_compare_fusion
  52.7 16.1 %collective-permute-done.2 = bf16[3,2048,128]{2,1,0:T(8,128)(2,1)} collective-permute-done((bf16[3,2048,128]{2,1,0:T(8,128)(2,1)}, bf16[3,2048,128]{2,1,0:T(8,128)(2,1)}, u32[]{:S(2)}, u32[]{:S(2)}) %collective-permute-start.2) | collective-permute-done | bytes 1572896 | tf_op jit(solution)/shard_map/ppermute | solution.py:15
  68.8 1.5 constant_dynamic-update-slice_fusion.7
  70.3 1.6 constant_dynamic-update-slice_fusion.6
  71.9 0.2 constant_dynamic-update-slice_fusion.5
  72.1 0.0 copy-done
  72.1 0.2 constant_dynamic-update-slice_fusion.4
  72.3 1.6 constant_dynamic-update-slice_fusion.3
  73.9 1.6 constant_dynamic-update-slice_fusion.2
  75.6 0.2 constant_dynamic-update-slice_fusion.1
  75.8 0.2 constant_dynamic-update-slice_fusion
  76.0 3.1 %constant_dynamic-slice_fusion = bf16[12,2048,128]{2,1,0:T(8,128)(2,1)} fusion(bf16[24,2048,128]{2,1,0:T(8,128)(2,1)S(1)} %constant_dynamic-update-slice_fusion, s32[]{:T(128)S(6)} %select_n.30), kind=kLoop, calls=%fused_computation.44 | loop fusion | bytes 12582916 | tf_op jit(solution)/shard_map/jit(_roll_dynamic)/dynamic_slice | solution.py:19
  79.1 5.6 %gather_fusion = bf16[6,2048,128]{2,1,0:T(8,128)(2,1)} fusion(bf16[12,2048,128]{2,1,0:T(8,128)(2,1)} %constant_dynamic-slice_fusion, s32[1024]{0:T(1024)S(1)} %pad_clamp_fusion), kind=kCustom, calls=%fused_computation | custom fusion | bytes 6291480 | tf_op jit(solution)/shard_map/gather | solution.py:53
  84.7 5.1 %broadcast_select_fusion = (bf16[6,2048,128]{2,1,0:T(8,128)(2,1)}, bf16[6,2048,128]{2,1,0:T(8,128)(2,1)S(1)}) fusion(pred[6]{0:T(512)(128)(4,1)S(1)} %broadcast_compare_fusion, bf16[6,2048,128]{2,1,0:T(8,128)(2,1)} %gather_fusion, f32[6,2048]{1,0:T(8,128)S(1)} %exp.3), kind=kLoop, calls=%fused_computation.11 | loop fusion | flops 6291456 | bytes 9486342 | tf_op jit(solution)/shard_map/jit(_where)/select_n | solution.py:54
  89.8 4.7 %copy.17 = f32[6,128,128]{0,2,1:T(8,128)} copy(f32[6,128,128]{2,1,0:T(8,128)S(1)} %slice_convert_fusion) | data formatting | bytes 786432 | tf_op jit(solution)/shard_map/slice | solution.py:25
  94.5 1.8 %gather_fusion.1 = f32[128,6]{1,0:T(8,128)S(1)} fusion(f32[6,128,128]{0,2,1:T(8,128)} %copy.17, s32[128]{0:T(128)S(1)} %or_bitcast_fusion), kind=kCustom, calls=%fused_computation.1 | custom fusion | bytes 7168 | tf_op jit(solution)/shard_map/jit(diagonal)/gather | solution.py:27
  96.3 0.1 copy.18
  96.3 1.3 convolution_subtract_fusion.2
  97.6 1.4 fusion.5
  99.0 1.2 convolution_subtract_fusion.1
  100.2 0.5 fusion.17
  100.7 1.2 convolution_subtract_fusion
  101.9 0.5 fusion.18
  102.4 4.0 %convolution_convert_fusion = bf16[6,2048,128]{2,1,0:T(8,128)(2,1)} fusion(bf16[6,2048,128]{2,1,0:T(8,128)(2,1)S(1)} %get-tuple-element.7, f32[6,128,128]{2,1,0:T(8,128)S(1)} %fusion.18), kind=kOutput, calls=%fused_computation.9 | convolution fusion | flops 2417491968 | bytes 6684672 | tf_op jit(solution)/shard_map/wnk,wkj->wnj/dot_general | solution.py:37
  106.4 31.4 %all-gather.2.cloned.1.call-done = bf16[16,128,2048]{2,1,0:T(8,128)(2,1)} async-done(((bf16[2,128,2048]{2,1,0:T(8,128)(2,1)}), bf16[16,128,2048]{2,1,0:T(8,128)(2,1)}) %all-gather.2.cloned.1.call-update) | async-done | bytes 8388624 | tf_op jit(solution)/shard_map/all_gather | solution.py:57
  137.8 11.7 %fusion = f32[6,128,16,128]{3,1,2,0:T(8,128)} fusion(bf16[16,128,2048]{2,1,0:T(8,128)(2,1)} %all-gather.2.cloned.1.call-done, bf16[6,2048,128]{2,1,0:T(8,128)(2,1)} %convolution_convert_fusion), kind=kOutput, calls=%fused_computation.2 | convolution fusion | flops 6442450944 | bytes 17825792 | tf_op jit(solution)/shard_map/gin,wnj->wgij/dot_general | solution.py:42
  149.5 0.0 copy-start.1
  149.5 6.6 %copy.20 = f32[6,128,16,128]{1,3,2,0:T(8,128)} copy(f32[6,128,16,128]{3,1,2,0:T(8,128)} %fusion) | data formatting | bytes 12582912 | tf_op jit(solution)/shard_map/gin,wnj->wgij/dot_general | solution.py:42
  156.1 0.0 copy-done.1
  156.1 0.0 copy-start.2
  156.1 5.9 %fusion.3 = (f32[6,16]{1,0:T(8,128)S(1)}, f32[6,16]{1,0:T(8,128)S(1)}) fusion(f32[6,128,16,128]{1,3,2,0:T(8,128)} %copy.20, pred[128,128]{1,0:T(8,128)(4,1)S(1)} %copy-done.1, f32[6,128,16,128]{3,1,2,0:T(8,128)} %fusion), kind=kLoop, calls=%fused_computation.7 | loop fusion | flops 6291264 | bytes 12600064 | tf_op jit(solution)/shard_map/wgii->wg/reduce_sum | solution.py:43
  162.0 0.1 subtract_reduce_fusion
  162.1 0.0 copy-done.2
  162.1 0.5 multiply_select_fusion
  (3 shorter events, 0.0 us)
Async XLA Ops:
  7.2 64.9 %copy-start = (bf16[3,2048,128]{2,1,0:T(8,128)(2,1)S(1)}, bf16[3,2048,128]{2,1,0:T(8,128)(2,1)}, u32[]{:S(2)}) copy-start(bf16[3,2048,128]{2,1,0:T(8,128)(2,1)} %param.4) | copy-start | bytes 4718596
  7.2 130.6 %all-gather.2.cloned.1.call-start = ((), (), s32[]{:S(2)}) async-start(), calls=%async_computation | async-start | bytes 9437184 | tf_op jit(solution)/shard_map/all_gather | solution.py:57
  7.9 20.7 %collective-permute-start = (bf16[3,2048,128]{2,1,0:T(8,128)(2,1)}, bf16[3,2048,128]{2,1,0:T(8,128)(2,1)S(1)}, u32[]{:S(2)}, u32[]{:S(2)}) collective-permute-start(bf16[3,2048,128]{2,1,0:T(8,128)(2,1)} %param.4), channel_id=1, source_target_pairs={{0,8},{8,16},{16,24},{24,0},{1,9},{9,17},{17,25},{25,1},{2,10},{10... | collective-permute-start | bytes 4718600 | tf_op jit(solution)/shard_map/ppermute | solution.py:15
  28.6 19.9 %collective-permute-start.1 = (bf16[3,2048,128]{2,1,0:T(8,128)(2,1)S(1)}, bf16[3,2048,128]{2,1,0:T(8,128)(2,1)}, u32[]{:S(2)}, u32[]{:S(2)}) collective-permute-start(bf16[3,2048,128]{2,1,0:T(8,128)(2,1)S(1)} %collective-permute-done), channel_id=1, source_target_pairs={{0,8},{8,16},{16,24},{24,0},{1,9},{9,17},{17,25},{25,1},{2,10},{10... | collective-permute-start | bytes 4718600 | tf_op jit(solution)/shard_map/ppermute | solution.py:15
  48.6 20.2 %collective-permute-start.2 = (bf16[3,2048,128]{2,1,0:T(8,128)(2,1)}, bf16[3,2048,128]{2,1,0:T(8,128)(2,1)}, u32[]{:S(2)}, u32[]{:S(2)}) collective-permute-start(bf16[3,2048,128]{2,1,0:T(8,128)(2,1)} %collective-permute-done.1), channel_id=1, source_target_pairs={{0,8},{8,16},{16,24},{24,0},{1,9},{9,17},{17,25},{25,1},{2,10},{10... | collective-permute-start | bytes 4718600 | tf_op jit(solution)/shard_map/ppermute | solution.py:15
  149.5 6.6 %copy-start.1 = (pred[128,128]{1,0:T(8,128)(4,1)S(1)}, pred[128,128]{1,0:T(8,128)(4,1)}, u32[]{:S(2)}) copy-start(pred[128,128]{1,0:T(8,128)(4,1)} %iota_compare_fusion.1) | copy-start | bytes 49156
  156.1 6.0 %copy-start.2 = (s32[6]{0:T(128)S(1)}, s32[6]{0:T(128)}, u32[]{:S(2)}) copy-start(s32[6]{0:T(128)} %param.6) | copy-start | bytes 76
Sparse Core Ops, SparseCore 0:
  10.1 127.6 all-gather.1
